TPU v7x, 32 devices: a whole 2x2x4 slice. The times are simulated.
32 devices in a mesh: tm: 2 (over x), prow: 4 (over z), pcol: 4 (over y, core).
Axes of the slice: x: 2, y: 2, z: 4, core: 2. Of those that a mesh axis runs over, the one named last changes fastest.
Arguments:
- signal: bfloat16 [2048, 15360], P(('prow', 'pcol'), 'tm'), may hold values from -8 to 8
- offsets: int32 [4], replicated, may hold values from 0 to 511, as said below
- pair_list: int32 [4, 4, 4, 2], P('prow', 'pcol'), may hold values from 0 to 3, as said below
Outputs:
- correlations: bfloat16 [4, 4, 4, 128, 128, 256], P('prow', 'pcol', None, 'tm')
Inputs may be any that keep to these rules, and one draw needn't show every extreme that they name: `offsets`: some window has the largest offset. `pair_list`: entry (a, b) of cell (r, c) pairs row block r n + a with column block b n + c, n the number of devices of pcol, and the row block's number is never above the column block's; pairs may repeat.
All inputs are finite; a program needn't handle non-finite values.
Results may differ from a plain program's by a relative error of at most 0.0058.
Values may be sent and summed in bfloat16 or wider, within the bound.
No kernel may reach another device: no remote copies, remote signals or barrier semaphores. Data moves between devices by JAX's collectives and lax.ppermute only.
A program may use at most 128 MiB of HBM per device.

v0:
```python
import math
import jax
import jax.numpy as jnp
from jax import lax
from jax.sharding import PartitionSpec as P

WIN = 7680
NF = 384
K0 = 32
LAGS = 256
SPAN = 4
NP = 4
STEP = 3840
HALO = 4352
two_pi = 2.0 * math.pi


def from_behind(value, axis, steps):
    count = lax.axis_size(axis)
    initial, last = (max(0, -steps), min(count, count - steps))
    return lax.ppermute(value, axis, [(source, source + steps) for source in range(initial, last)])


def forward_table():
    sample_idx = jnp.arange(WIN, dtype=jnp.int32)
    freq_bins = K0 + jnp.arange(NF, dtype=jnp.int32)
    wrapped = sample_idx[:, None] * freq_bins[None, :] % WIN
    phase_angle = wrapped.astype(jnp.float32) * (two_pi / WIN)
    taper_curve = 0.5 - 0.5 * jnp.cos(sample_idx.astype(jnp.float32) * (two_pi / WIN))
    cosine = taper_curve[:, None] * jnp.cos(phase_angle)
    sine = -taper_curve[:, None] * jnp.sin(phase_angle)
    return jnp.concatenate([cosine, sine], axis=1).astype(jnp.bfloat16)


def lag_table(count):
    freq_bins = K0 + jnp.arange(NF, dtype=jnp.int32)
    shifted = (jnp.arange(LAGS, dtype=jnp.int32) - LAGS // 2) % WIN
    wrapped = freq_bins[:, None] * shifted[None, :] % WIN
    phase_angle = wrapped.astype(jnp.float32) * (two_pi / WIN)
    factor = 1.0 / math.sqrt(NF * count)
    return jnp.concatenate(
        [jnp.cos(phase_angle) * factor, -jnp.sin(phase_angle) * factor], axis=0
    ).astype(jnp.bfloat16)


def whiten(spectra):
    real_part = spectra[..., :NF]
    imag_part = spectra[..., NF:]
    power_sum = real_part * real_part + imag_part * imag_part
    freq_bins = jnp.arange(NF, dtype=jnp.int32)
    band_matrix = (jnp.abs(freq_bins[:, None] - freq_bins[None, :]) <= SPAN).astype(jnp.float32)
    smooth = jnp.einsum(
        "...f,fg->...g", power_sum, band_matrix, precision=lax.Precision.HIGHEST
    ) / (2 * SPAN + 1)
    water_level = jnp.mean(power_sum, axis=-1, keepdims=True)
    weight = lax.rsqrt(smooth + 0.5 * water_level + 1e-06)
    return (spectra * jnp.concatenate([weight, weight], axis=-1)).astype(jnp.bfloat16)


def cross_pair(row_block, col_block, lags):
    row_real = row_block[..., :NF]
    row_imag = row_block[..., NF:]
    col_both = jnp.concatenate([col_block[..., :NF], col_block[..., NF:]], axis=0)
    row_first = jnp.concatenate([row_real, row_imag], axis=0)
    row_second = jnp.concatenate([row_imag, -row_real], axis=0)
    real_sum = jnp.einsum("wif,wjf->ijf", row_first, col_both, preferred_element_type=jnp.float32)
    imag_sum = jnp.einsum("wif,wjf->ijf", row_second, col_both, preferred_element_type=jnp.float32)
    cross = jnp.concatenate([real_sum, imag_sum], axis=-1).astype(jnp.bfloat16)
    flat = cross.reshape(-1, 2 * NF)
    result = jnp.dot(flat, lags, preferred_element_type=jnp.float32).astype(jnp.bfloat16)
    return result.reshape(row_block.shape[1], col_block.shape[1], LAGS)


def on_device(signal, offsets, pair_list):
    channels_here = signal.shape[0]
    samples_here = signal.shape[1]
    w_dev = samples_here // STEP
    n_tm = lax.axis_size("tm")
    tm_index = lax.axis_index("tm")
    dft_table = forward_table()
    head_samples = signal[:, :HALO]
    next_head = from_behind(head_samples, "tm", -1)
    extended = jnp.concatenate([signal, next_head], axis=1)

    def one_window(window):
        first_sample = window * STEP + offsets[tm_index * w_dev + window]
        segment = lax.dynamic_slice_in_dim(extended, first_sample, WIN, 1)
        return jnp.dot(segment, dft_table, preferred_element_type=jnp.float32)

    spectra = lax.map(one_window, jnp.arange(w_dev, dtype=jnp.int32))
    whitened = whiten(spectra)
    own_piece = whitened[None]
    row_gathered = lax.all_gather(own_piece, ("tm", "pcol"), axis=0, tiled=True)
    col_gathered = lax.all_gather(own_piece, ("tm", "prow"), axis=0, tiled=True)
    row_gathered = row_gathered.reshape(n_tm, -1, w_dev, channels_here, 2 * NF)
    col_gathered = col_gathered.reshape(n_tm, -1, w_dev, channels_here, 2 * NF)
    pick_dim = 1
    lags = lag_table(n_tm * w_dev)
    local_pairs = pair_list[0, 0]
    half_rows = channels_here // n_tm
    first_row = tm_index * half_rows

    def one_pair(pair_index):
        row_pick = local_pairs[pair_index, 0]
        col_pick = local_pairs[pair_index, 1]
        row_whole = lax.dynamic_index_in_dim(row_gathered, row_pick, pick_dim, keepdims=False)
        col_whole = lax.dynamic_index_in_dim(col_gathered, col_pick, pick_dim, keepdims=False)
        row_whole = row_whole.reshape(n_tm * w_dev, channels_here, 2 * NF)
        col_whole = col_whole.reshape(n_tm * w_dev, channels_here, 2 * NF)
        row_block = lax.dynamic_slice_in_dim(row_whole, first_row, half_rows, 1)
        return cross_pair(row_block, col_whole, lags)

    result = lax.map(one_pair, jnp.arange(NP, dtype=jnp.int32))
    return result.reshape(1, 1, NP, half_rows, channels_here, LAGS)


def solution(mesh):
    placed = (P(("prow", "pcol"), "tm"), P(), P("prow", "pcol", None, None))
    return jax.shard_map(
        on_device,
        mesh=mesh,
        in_specs=placed,
        out_specs=P("prow", "pcol", None, "tm", None, None),
        check_vma=False,
    )
```

profile of v0, /device:TPU:0, one launch (start us, length us, event | category | flops | bytes accessed | tf_op | source)
XLA Modules:
  0.0 409.1 jit_solution(12209533261240623052)
XLA Ops:
  9.3 52.4 %multiply_convert_fusion.1 = (bf16[7680,384]{1,0:T(8,128)(2,1)S(1)}, bf16[7680,384]{1,0:T(8,128)(2,1)S(1)}) fusion(s32[384]{0:T(512)S(1)} %iota_add_fusion, f32[7680]{0:T(1024)S(1)} %get-tuple-element.245, f32[7680]{0:T(1024)S(1)} %get-tuple-element.246), kind=kLoop, calls=%fused_computation.36 | loop fusion | flops 38338560 | bytes 11859456 | tf_op jit(solution)/shard_map/convert.8
  61.8 5.0 %pad_maximum_fusion.3 = bf16[7680,768]{1,0:T(8,128)(2,1)} fusion(bf16[7680,384]{1,0:T(8,128)(2,1)S(1)} %get-tuple-element.244, bf16[7680,384]{1,0:T(8,128)(2,1)S(1)} %get-tuple-element.243), kind=kLoop, calls=%fused_computation.34 | loop fusion | flops 23592960 | bytes 23592960 | tf_op jit(solution)/shard_map/concatenate | solution.py:32
  68.2 19.9 %while.24 = (s32[]{:T(128)}, f32[2,128,768]{2,1,0:T(8,128)}, s32[2]{0:T(128)S(1)}, s32[]{:T(128)}, s32[4]{0:T(128)S(1)}, /*index=5*/bf16[128,12032]{1,0:T(8,128)...) while((s32[]{:T(128)}, f32[2,128,768]{2,1,0:T(8,128)}, ...), condition=%wide.region_1.2_spmd, body=%wide.region_0.1_spmd.sunk | while | flops 1509949440 | bytes 14156537 | solution.py:90
  71.2 7.0 %fusion.61 = f32[2,128,768]{2,1,0:T(8,128)} fusion(f32[2,128,768]{2,1,0:T(8,128)} %get-tuple-element.370, s32[]{:T(128)} %get-tuple-element.369, bf16[7680,768]{1,0:T(8,128)(2,1)} %get-tuple-element.387, bf16[128,12032]{1,0:T(8,128)(2,1)S(1)} %get-tuple-element.386, s32[]{:T(128)S(6)} %select_n.90), kind=kOutput, calls=%fused_computation.3.clone.1 | convolution fusion | flops 1509949440 | bytes 14156292 | tf_op jit(solution)/shard_map/while/body/eval_jaxpr/dot_general | solution.py:88
  81.2 6.9 %fusion.61 = f32[2,128,768]{2,1,0:T(8,128)} fusion(f32[2,128,768]{2,1,0:T(8,128)} %get-tuple-element.370, s32[]{:T(128)} %get-tuple-element.369, bf16[7680,768]{1,0:T(8,128)(2,1)} %get-tuple-element.387, bf16[128,12032]{1,0:T(8,128)(2,1)S(1)} %get-tuple-element.386, s32[]{:T(128)S(6)} %select_n.90), kind=kOutput, calls=%fused_computation.3.clone.1 | convolution fusion | flops 1509949440 | bytes 14156292 | tf_op jit(solution)/shard_map/while/body/eval_jaxpr/dot_general | solution.py:88
  95.9 62.2 %all-gather.5.cloned.1.call-done = bf16[16,128,768]{2,1,0:T(8,128)(2,1)} async-done(((bf16[2,128,768]{2,1,0:T(8,128)(2,1)}), bf16[16,128,768]{2,1,0:T(8,128)(2,1)}) %all-gather.5.cloned.1.call-update) | async-done | bytes 3145744 | tf_op jit(solution)/shard_map/all_gather | solution.py:94
  158.1 32.8 %all-gather.7.cloned.1.call-done = bf16[16,128,768]{2,1,0:T(8,128)(2,1)} async-done(((bf16[2,128,768]{2,1,0:T(8,128)(2,1)}), bf16[16,128,768]{2,1,0:T(8,128)(2,1)}) %all-gather.7.cloned.1.call-update) | async-done | bytes 3145744 | tf_op jit(solution)/shard_map/all_gather | solution.py:93
  190.9 211.1 %while.25 = (s32[]{:T(128)}, bf16[4,64,128,256]{3,2,1,0:T(8,128)(2,1)}, s32[4]{0:T(128)S(1)}, s32[4,2]{0,1:T(2,128)S(1)}, bf16[2,4,2,128,768]{4,3,2,1,0:T(8,128)...) while((s32[]{:T(128)}, ...), condition=%wide.region_4.5_spmd, body=%wide.region_3.4_spmd.sunk | while | flops 3360456704 | bytes 74515224 | solution.py:113
  224.5 12.5 %copy.23 = bf16[48,8,64,128]{3,1,2,0:T(8,128)(2,1)S(1)} copy(bf16[48,8,64,128]{3,2,1,0:T(8,128)(2,1)S(1)} %bitcast.66) | data formatting | bytes 12582912 | tf_op jit(solution)/shard_map/while
  239.1 12.5 %copy.22 = bf16[48,8,64,128]{3,1,2,0:T(8,128)(2,1)S(1)} copy(bf16[48,8,64,128]{3,2,1,0:T(8,128)(2,1)S(1)} %bitcast.65) | data formatting | bytes 12582912 | tf_op jit(solution)/shard_map/while
  251.6 5.6 %fusion.68 = bf16[8192,256]{1,0:T(8,128)(2,1)S(1)} fusion(bf16[768,256]{1,0:T(8,128)(2,1)S(1)} %get-tuple-element.424, bf16[8192,384]{0,1:T(8,128)(2,1)S(1)} %bitcast.68, bf16[8192,384]{0,1:T(8,128)(2,1)S(1)} %bitcast.67), kind=kOutput, calls=%fused_computation.9.clone.1 | convolution fusion | flops 3248488448 | bytes 17170432 | tf_op jit(solution)/shard_map/while/body/eval_jaxpr/dot_general | solution.py:70
  257.2 2.3 constant_dynamic-update-slice_fusion.2
  272.0 12.5 %copy.23 = bf16[48,8,64,128]{3,1,2,0:T(8,128)(2,1)S(1)} copy(bf16[48,8,64,128]{3,2,1,0:T(8,128)(2,1)S(1)} %bitcast.66) | data formatting | bytes 12582912 | tf_op jit(solution)/shard_map/while
  286.6 12.5 %copy.22 = bf16[48,8,64,128]{3,1,2,0:T(8,128)(2,1)S(1)} copy(bf16[48,8,64,128]{3,2,1,0:T(8,128)(2,1)S(1)} %bitcast.65) | data formatting | bytes 12582912 | tf_op jit(solution)/shard_map/while
  299.1 5.6 %fusion.68 = bf16[8192,256]{1,0:T(8,128)(2,1)S(1)} fusion(bf16[768,256]{1,0:T(8,128)(2,1)S(1)} %get-tuple-element.424, bf16[8192,384]{0,1:T(8,128)(2,1)S(1)} %bitcast.68, bf16[8192,384]{0,1:T(8,128)(2,1)S(1)} %bitcast.67), kind=kOutput, calls=%fused_computation.9.clone.1 | convolution fusion | flops 3248488448 | bytes 17170432 | tf_op jit(solution)/shard_map/while/body/eval_jaxpr/dot_general | solution.py:70
  304.7 2.3 constant_dynamic-update-slice_fusion.2
  319.5 12.5 %copy.23 = bf16[48,8,64,128]{3,1,2,0:T(8,128)(2,1)S(1)} copy(bf16[48,8,64,128]{3,2,1,0:T(8,128)(2,1)S(1)} %bitcast.66) | data formatting | bytes 12582912 | tf_op jit(solution)/shard_map/while
  334.1 12.5 %copy.22 = bf16[48,8,64,128]{3,1,2,0:T(8,128)(2,1)S(1)} copy(bf16[48,8,64,128]{3,2,1,0:T(8,128)(2,1)S(1)} %bitcast.65) | data formatting | bytes 12582912 | tf_op jit(solution)/shard_map/while
  346.6 5.6 %fusion.68 = bf16[8192,256]{1,0:T(8,128)(2,1)S(1)} fusion(bf16[768,256]{1,0:T(8,128)(2,1)S(1)} %get-tuple-element.424, bf16[8192,384]{0,1:T(8,128)(2,1)S(1)} %bitcast.68, bf16[8192,384]{0,1:T(8,128)(2,1)S(1)} %bitcast.67), kind=kOutput, calls=%fused_computation.9.clone.1 | convolution fusion | flops 3248488448 | bytes 17170432 | tf_op jit(solution)/shard_map/while/body/eval_jaxpr/dot_general | solution.py:70
  352.2 2.3 constant_dynamic-update-slice_fusion.2
  366.9 12.5 %copy.23 = bf16[48,8,64,128]{3,1,2,0:T(8,128)(2,1)S(1)} copy(bf16[48,8,64,128]{3,2,1,0:T(8,128)(2,1)S(1)} %bitcast.66) | data formatting | bytes 12582912 | tf_op jit(solution)/shard_map/while
  381.6 12.5 %copy.22 = bf16[48,8,64,128]{3,1,2,0:T(8,128)(2,1)S(1)} copy(bf16[48,8,64,128]{3,2,1,0:T(8,128)(2,1)S(1)} %bitcast.65) | data formatting | bytes 12582912 | tf_op jit(solution)/shard_map/while
  394.1 5.6 %fusion.68 = bf16[8192,256]{1,0:T(8,128)(2,1)S(1)} fusion(bf16[768,256]{1,0:T(8,128)(2,1)S(1)} %get-tuple-element.424, bf16[8192,384]{0,1:T(8,128)(2,1)S(1)} %bitcast.68, bf16[8192,384]{0,1:T(8,128)(2,1)S(1)} %bitcast.67), kind=kOutput, calls=%fused_computation.9.clone.1 | convolution fusion | flops 3248488448 | bytes 17170432 | tf_op jit(solution)/shard_map/while/body/eval_jaxpr/dot_general | solution.py:70
  399.6 2.3 constant_dynamic-update-slice_fusion.2
  (67 shorter events, 50.9 us)
Async XLA Ops:
  6.5 151.5 %all-gather.5.cloned.1.call-start = ((), (), s32[]{:S(2)}) async-start(), calls=%async_computation | async-start | bytes 3538944 | tf_op jit(solution)/shard_map/all_gather | solution.py:94
  7.9 58.9 %collective-permute-start = (bf16[128,4352]{1,0:T(8,128)(2,1)S(1)}, bf16[128,4352]{1,0:T(8,128)(2,1)}, u32[]{:S(2)}, u32[]{:S(2)}) collective-permute-start(bf16[128,4352]{1,0:T(8,128)(2,1)S(1)} %slice.29), channel_id=1, source_target_pairs={{16,0},{17,1},{18,2},{19,3},{20,4},{21,5},{22,6},{23,7},{24,8},{25... | collective-permute-start | bytes 3342344 | tf_op jit(solution)/shard_map/ppermute | solution.py:21
  61.8 5.0 %copy-start = (bf16[128,7680]{1,0:T(8,128)(2,1)S(1)}, bf16[128,7680]{1,0:T(8,128)(2,1)}, u32[]{:S(2)}) copy-start(bf16[128,7680]{1,0:T(8,128)(2,1)} %param.7) | copy-start | bytes 5898244
  61.8 6.4 %copy-start.2 = (s32[4]{0:T(128)S(1)}, s32[4]{0:T(128)}, u32[]{:S(2)}) copy-start(s32[4]{0:T(128)} %param.8) | copy-start | bytes 52
  68.2 122.6 %copy-start.1 = (s32[1,1,4,2]{2,3,1,0:T(2,128)S(1)}, s32[1,1,4,2]{2,3,1,0:T(2,128)}, u32[]{:S(2)}) copy-start(s32[1,1,4,2]{2,3,1,0:T(2,128)} %param.9) | copy-start | bytes 100
  93.1 97.7 %all-gather.7.cloned.1.call-start = ((), (), s32[]{:S(2)}) async-start(), calls=%async_computation.1 | async-start | bytes 3538944 | tf_op jit(solution)/shard_map/all_gather | solution.py:93
Sparse Core Ops, SparseCore 0:
  93.2 64.8 all-gather.4
  160.0 30.8 all-gather.6
where the time goes:
time: 415 us; the launch traced here: 409 us
  local copies, waits for them, and re-layouts  130 us (31%)
  waiting for transfers between devices  95.7 us (23%)
  other arithmetic  66.6 us (16%)
  matrix products  55.2 us (13%)
  loops' own time  46.9 us (11%)
  between operations  13.9 us (3%)
    while x8, local copies, waits for them, and re-layouts  99.7 us
    all_gather x1, waiting for transfers between devices, on_device(): col_gathered = lax.all_gather(own_piece, ('tm', 'prow'), axis=0, tiled=True)  62.2 us
    another operation x2, other arithmetic  54.4 us
    another operation x1, loops' own time, on_device(): result = lax.map(one_pair, jnp.arange(NP, dtype=jnp.int32))  43.2 us
    all_gather x1, waiting for transfers between devices, on_device(): row_gathered = lax.all_gather(own_piece, ('tm', 'pcol'), axis=0, tiled=True)  32.8 us
    dot_general x4, matrix products, cross_pair(): jnp.dot(flat, lags, preferred_element_type=jnp.float32).astype(jnp.bfloat16)  22.3 us
    dot_general x2, matrix products, one_window(): return jnp.dot(segment, dft_table, preferred_element_type=jnp.float32)  13.9 us
    dynamic_update_slice x4, local copies, waits for them, and re-layouts, on_device(): result = lax.map(one_pair, jnp.arange(NP, dtype=jnp.int32))  9.16 us
  transfers between devices with their start and end apart: 3, of which 2 were waited for; matrix products, arithmetic and copies ran while one was open for 15% of the time, Pallas kernels for 0%

commit v1 on v0

--- a/solution.py
+++ b/solution.py
@@ -13,6 +13,12 @@
 STEP = 3840
 HALO = 4352
 two_pi = 2.0 * math.pi
+
+
+def laid_out(tiles, dim):
+    tiles = jnp.moveaxis(tiles, 0, dim)
+    shape = tiles.shape
+    return tiles.reshape(*shape[:dim], shape[dim] * shape[dim + 1], *shape[dim + 2 :])
 
 
 def from_behind(value, axis, steps):
@@ -90,7 +96,19 @@
     spectra = lax.map(one_window, jnp.arange(w_dev, dtype=jnp.int32))
     whitened = whiten(spectra)
     own_piece = whitened[None]
-    row_gathered = lax.all_gather(own_piece, ("tm", "pcol"), axis=0, tiled=True)
+    size = lax.axis_size(("tm", "pcol"))
+    pairs = [(i, (i + 1) % size) for i in range(size)]
+    back = [(b, a) for a, b in pairs]
+    lower, upper = ([], [])
+    for step in range(size - 1):
+        if step % 2 == 0:
+            lower.append(lax.ppermute(lower[-1] if lower else own_piece, ("tm", "pcol"), pairs))
+        else:
+            upper.append(lax.ppermute(upper[-1] if upper else own_piece, ("tm", "pcol"), back))
+    blocks = jnp.stack([*lower[::-1], own_piece, *upper])
+    shift = lax.axis_index(("tm", "pcol")) - len(lower)
+    blocks = blocks[(jnp.arange(size) - shift) % size]
+    row_gathered = laid_out(blocks, 0)
     col_gathered = lax.all_gather(own_piece, ("tm", "prow"), axis=0, tiled=True)
     row_gathered = row_gathered.reshape(n_tm, -1, w_dev, channels_here, 2 * NF)
     col_gathered = col_gathered.reshape(n_tm, -1, w_dev, channels_here, 2 * NF)

time: 415 us -> 390 us (0.940)
  waiting for transfers between devices: 95.7 us -> 48.9 us
  local copies, waits for them, and re-layouts: 130 us -> 140 us
  starting transfers between devices: 1.34 us -> 9.88 us
    all_gather x1, waiting for transfers between devices: 62.2 us -> 15.7 us  [on_device(): col_gathered = lax.all_gather(own_piece, ('tm', 'prow'), axis=0, tiled=True)]
    ppermute x0 -> x7, waiting for transfers between devices: none -> 33.2 us  [the longest x4 33.2 us: on_device(): lax.ppermute(lower[-1] if lower else own_piece, ('tm', 'pcol'), pairs)]
    all_gather x1 -> x0, waiting for transfers between devices: 32.8 us -> none  [on_device(): row_gathered = lax.all_gather(own_piece, ('tm', 'pcol'), axis=0, tiled=True)]
    ppermute x0 -> x7, starting transfers between devices: none -> 8.58 us  [the longest x3 8.03 us: on_device(): lax.ppermute(upper[-1] if upper else own_piece, ('tm', 'pcol'), back)]
    unnamed x6 -> x21, local copies, waits for them, and re-layouts: 0.02 us -> 7.95 us
  transfers between devices with their start and end apart: 3 -> 9, of which waited for: 2 -> 5; matrix products, arithmetic and copies ran while one was open for 15% -> 18% of each run, Pallas kernels for 0% -> 0%
where the time goes in v1:
time: 390 us; the launch traced here: 383 us
  local copies, waits for them, and re-layouts  140 us (36%)
  other arithmetic  66.6 us (17%)
  matrix products  55.1 us (14%)
  waiting for transfers between devices  48.9 us (13%)
  loops' own time  48.2 us (12%)
  between operations  14 us (4%)
  starting transfers between devices  9.88 us (3%)
    while x8, local copies, waits for them, and re-layouts  99.7 us
    another operation x2, other arithmetic  54.4 us
    another operation x1, loops' own time, on_device(): result = lax.map(one_pair, jnp.arange(NP, dtype=jnp.int32))  44.2 us
    ppermute x4, waiting for transfers between devices, on_device(): lax.ppermute(lower[-1] if lower else own_piece, ('tm', 'pcol'), pairs)  33.2 us
    dot_general x4, matrix products, cross_pair(): jnp.dot(flat, lags, preferred_element_type=jnp.float32).astype(jnp.bfloat16)  22.2 us
    all_gather x1, waiting for transfers between devices, on_device(): col_gathered = lax.all_gather(own_piece, ('tm', 'prow'), axis=0, tiled=True)  15.7 us
    dot_general x2, matrix products, one_window(): return jnp.dot(segment, dft_table, preferred_element_type=jnp.float32)  13.9 us
    dynamic_update_slice x4, local copies, waits for them, and re-layouts, on_device(): result = lax.map(one_pair, jnp.arange(NP, dtype=jnp.int32))  9.16 us
  transfers between devices with their start and end apart: 9, of which 5 were waited for; matrix products, arithmetic and copies ran while one was open for 18% of the time, Pallas kernels for 0%

profile of v1, /device:TPU:0, one launch (start us, length us, event | category | flops | bytes accessed | tf_op | source)
XLA Modules:
  0.0 382.6 jit_solution(3329999451369405715)
XLA Ops:
  9.3 52.4 %multiply_convert_fusion.1 = (bf16[7680,384]{1,0:T(8,128)(2,1)S(1)}, bf16[7680,384]{1,0:T(8,128)(2,1)S(1)}) fusion(s32[384]{0:T(512)S(1)} %iota_add_fusion, f32[7680]{0:T(1024)S(1)} %get-tuple-element.245, f32[7680]{0:T(1024)S(1)} %get-tuple-element.246), kind=kLoop, calls=%fused_computation.37 | loop fusion | flops 38338560 | bytes 11859456 | tf_op jit(solution)/shard_map/convert.8
  61.8 5.0 %pad_maximum_fusion.3 = bf16[7680,768]{1,0:T(8,128)(2,1)} fusion(bf16[7680,384]{1,0:T(8,128)(2,1)S(1)} %get-tuple-element.244, bf16[7680,384]{1,0:T(8,128)(2,1)S(1)} %get-tuple-element.243), kind=kLoop, calls=%fused_computation.35 | loop fusion | flops 23592960 | bytes 23592960 | tf_op jit(solution)/shard_map/concatenate | solution.py:38
  68.2 20.4 %while.24 = (s32[]{:T(128)}, f32[2,128,768]{2,1,0:T(8,128)}, s32[2]{0:T(128)S(1)}, s32[]{:T(128)}, s32[4]{0:T(128)S(1)}, /*index=5*/bf16[128,12032]{1,0:T(8,128)...) while((s32[]{:T(128)}, f32[2,128,768]{2,1,0:T(8,128)}, ...), condition=%wide.region_1.2_spmd, body=%wide.region_0.1_spmd.sunk | while | flops 1509949440 | bytes 14156537 | solution.py:96
  71.4 7.0 %fusion.63 = f32[2,128,768]{2,1,0:T(8,128)} fusion(f32[2,128,768]{2,1,0:T(8,128)} %get-tuple-element.370, s32[]{:T(128)} %get-tuple-element.369, bf16[7680,768]{1,0:T(8,128)(2,1)} %get-tuple-element.387, bf16[128,12032]{1,0:T(8,128)(2,1)S(1)} %get-tuple-element.386, s32[]{:T(128)S(6)} %select_n.123), kind=kOutput, calls=%fused_computation.4.clone.1 | convolution fusion | flops 1509949440 | bytes 14156292 | tf_op jit(solution)/shard_map/while/body/eval_jaxpr/dot_general | solution.py:94
  81.6 7.0 %fusion.63 = f32[2,128,768]{2,1,0:T(8,128)} fusion(f32[2,128,768]{2,1,0:T(8,128)} %get-tuple-element.370, s32[]{:T(128)} %get-tuple-element.369, bf16[7680,768]{1,0:T(8,128)(2,1)} %get-tuple-element.387, bf16[128,12032]{1,0:T(8,128)(2,1)S(1)} %get-tuple-element.386, s32[]{:T(128)S(6)} %select_n.123), kind=kOutput, calls=%fused_computation.4.clone.1 | convolution fusion | flops 1509949440 | bytes 14156292 | tf_op jit(solution)/shard_map/while/body/eval_jaxpr/dot_general | solution.py:94
  94.1 10.4 %collective-permute-done.1 = bf16[1,2,128,768]{3,2,1,0:T(8,128)(2,1)S(1)} collective-permute-done((bf16[1,2,128,768]{3,2,1,0:T(8,128)(2,1)}, bf16[1,2,128,768]{3,2,1,0:T(8,128)(2,1)S(1)}, u32[]{:S(2)}, u32[]{:S(2)}) %collective-permute-start.1) | collective-permute-done | bytes 393248 | tf_op jit(solution)/shard_map/ppermute | solution.py:105
  107.8 9.7 %collective-permute-done.2 = bf16[1,2,128,768]{3,2,1,0:T(8,128)(2,1)S(1)} collective-permute-done((bf16[1,2,128,768]{3,2,1,0:T(8,128)(2,1)S(1)}, bf16[1,2,128,768]{3,2,1,0:T(8,128)(2,1)S(1)}, u32[]{:S(2)}, u32[]{:S(2)}) %collective-permute-start.2) | collective-permute-done | bytes 393248 | tf_op jit(solution)/shard_map/ppermute | solution.py:105
  117.6 2.7 collective-permute-start.6
  120.3 5.5 %collective-permute-done.3 = bf16[1,2,128,768]{3,2,1,0:T(8,128)(2,1)S(1)} collective-permute-done((bf16[1,2,128,768]{3,2,1,0:T(8,128)(2,1)S(1)}, bf16[1,2,128,768]{3,2,1,0:T(8,128)(2,1)S(1)}, u32[]{:S(2)}, u32[]{:S(2)}) %collective-permute-start.3) | collective-permute-done | bytes 393248 | tf_op jit(solution)/shard_map/ppermute | solution.py:105
  130.5 7.7 %collective-permute-done.4 = bf16[1,2,128,768]{3,2,1,0:T(8,128)(2,1)} collective-permute-done((bf16[1,2,128,768]{3,2,1,0:T(8,128)(2,1)S(1)}, bf16[1,2,128,768]{3,2,1,0:T(8,128)(2,1)}, u32[]{:S(2)}, u32[]{:S(2)}) %collective-permute-start.4) | collective-permute-done | bytes 393248 | tf_op jit(solution)/shard_map/ppermute | solution.py:105
  147.8 15.7 %all-gather.3.cloned.1.call-done = bf16[16,128,768]{2,1,0:T(8,128)(2,1)} async-done(((bf16[2,128,768]{2,1,0:T(8,128)(2,1)}), bf16[16,128,768]{2,1,0:T(8,128)(2,1)}) %all-gather.3.cloned.1.call-update) | async-done | bytes 3145744 | tf_op jit(solution)/shard_map/all_gather | solution.py:112
  163.6 211.8 %while.25 = (s32[]{:T(128)}, bf16[4,64,128,256]{3,2,1,0:T(8,128)(2,1)}, s32[4]{0:T(128)S(1)}, s32[4,2]{0,1:T(2,128)S(1)}, bf16[2,4,2,128,768]{4,3,2,1,0:T(8,128)...) while((s32[]{:T(128)}, ...), condition=%wide.region_4.5_spmd, body=%wide.region_3.4_spmd.sunk | while | flops 3360456704 | bytes 74515224 | solution.py:131
  197.4 12.5 %copy.23 = bf16[48,8,64,128]{3,1,2,0:T(8,128)(2,1)S(1)} copy(bf16[48,8,64,128]{3,2,1,0:T(8,128)(2,1)S(1)} %bitcast.86) | data formatting | bytes 12582912 | tf_op jit(solution)/shard_map/while
  212.0 12.5 %copy.22 = bf16[48,8,64,128]{3,1,2,0:T(8,128)(2,1)S(1)} copy(bf16[48,8,64,128]{3,2,1,0:T(8,128)(2,1)S(1)} %bitcast.85) | data formatting | bytes 12582912 | tf_op jit(solution)/shard_map/while
  224.5 5.6 %fusion.70 = bf16[8192,256]{1,0:T(8,128)(2,1)S(1)} fusion(bf16[768,256]{1,0:T(8,128)(2,1)S(1)} %get-tuple-element.424, bf16[8192,384]{0,1:T(8,128)(2,1)S(1)} %bitcast.88, bf16[8192,384]{0,1:T(8,128)(2,1)S(1)} %bitcast.87), kind=kOutput, calls=%fused_computation.10.clone.1 | convolution fusion | flops 3248488448 | bytes 17170432 | tf_op jit(solution)/shard_map/while/body/eval_jaxpr/dot_general | solution.py:76
  245.1 12.5 %copy.23 = bf16[48,8,64,128]{3,1,2,0:T(8,128)(2,1)S(1)} copy(bf16[48,8,64,128]{3,2,1,0:T(8,128)(2,1)S(1)} %bitcast.86) | data formatting | bytes 12582912 | tf_op jit(solution)/shard_map/while
  259.7 12.5 %copy.22 = bf16[48,8,64,128]{3,1,2,0:T(8,128)(2,1)S(1)} copy(bf16[48,8,64,128]{3,2,1,0:T(8,128)(2,1)S(1)} %bitcast.85) | data formatting | bytes 12582912 | tf_op jit(solution)/shard_map/while
  272.2 5.6 %fusion.70 = bf16[8192,256]{1,0:T(8,128)(2,1)S(1)} fusion(bf16[768,256]{1,0:T(8,128)(2,1)S(1)} %get-tuple-element.424, bf16[8192,384]{0,1:T(8,128)(2,1)S(1)} %bitcast.88, bf16[8192,384]{0,1:T(8,128)(2,1)S(1)} %bitcast.87), kind=kOutput, calls=%fused_computation.10.clone.1 | convolution fusion | flops 3248488448 | bytes 17170432 | tf_op jit(solution)/shard_map/while/body/eval_jaxpr/dot_general | solution.py:76
  292.8 12.5 %copy.23 = bf16[48,8,64,128]{3,1,2,0:T(8,128)(2,1)S(1)} copy(bf16[48,8,64,128]{3,2,1,0:T(8,128)(2,1)S(1)} %bitcast.86) | data formatting | bytes 12582912 | tf_op jit(solution)/shard_map/while
  307.4 12.5 %copy.22 = bf16[48,8,64,128]{3,1,2,0:T(8,128)(2,1)S(1)} copy(bf16[48,8,64,128]{3,2,1,0:T(8,128)(2,1)S(1)} %bitcast.85) | data formatting | bytes 12582912 | tf_op jit(solution)/shard_map/while
  319.9 5.6 %fusion.70 = bf16[8192,256]{1,0:T(8,128)(2,1)S(1)} fusion(bf16[768,256]{1,0:T(8,128)(2,1)S(1)} %get-tuple-element.424, bf16[8192,384]{0,1:T(8,128)(2,1)S(1)} %bitcast.88, bf16[8192,384]{0,1:T(8,128)(2,1)S(1)} %bitcast.87), kind=kOutput, calls=%fused_computation.10.clone.1 | convolution fusion | flops 3248488448 | bytes 17170432 | tf_op jit(solution)/shard_map/while/body/eval_jaxpr/dot_general | solution.py:76
  340.4 12.5 %copy.23 = bf16[48,8,64,128]{3,1,2,0:T(8,128)(2,1)S(1)} copy(bf16[48,8,64,128]{3,2,1,0:T(8,128)(2,1)S(1)} %bitcast.86) | data formatting | bytes 12582912 | tf_op jit(solution)/shard_map/while
  355.1 12.5 %copy.22 = bf16[48,8,64,128]{3,1,2,0:T(8,128)(2,1)S(1)} copy(bf16[48,8,64,128]{3,2,1,0:T(8,128)(2,1)S(1)} %bitcast.85) | data formatting | bytes 12582912 | tf_op jit(solution)/shard_map/while
  367.5 5.6 %fusion.70 = bf16[8192,256]{1,0:T(8,128)(2,1)S(1)} fusion(bf16[768,256]{1,0:T(8,128)(2,1)S(1)} %get-tuple-element.424, bf16[8192,384]{0,1:T(8,128)(2,1)S(1)} %bitcast.88, bf16[8192,384]{0,1:T(8,128)(2,1)S(1)} %bitcast.87), kind=kOutput, calls=%fused_computation.10.clone.1 | convolution fusion | flops 3248488448 | bytes 17170432 | tf_op jit(solution)/shard_map/while/body/eval_jaxpr/dot_general | solution.py:76
  (97 shorter events, 75.6 us)
Async XLA Ops:
  6.5 157.0 %all-gather.3.cloned.1.call-start = ((), (), s32[]{:S(2)}) async-start(), calls=%async_computation | async-start | bytes 3538944 | tf_op jit(solution)/shard_map/all_gather | solution.py:112
  7.9 58.9 %collective-permute-start = (bf16[128,4352]{1,0:T(8,128)(2,1)S(1)}, bf16[128,4352]{1,0:T(8,128)(2,1)}, u32[]{:S(2)}, u32[]{:S(2)}) collective-permute-start(bf16[128,4352]{1,0:T(8,128)(2,1)S(1)} %slice.29), channel_id=1, source_target_pairs={{16,0},{17,1},{18,2},{19,3},{20,4},{21,5},{22,6},{23,7},{24,8},{25... | collective-permute-start | bytes 3342344 | tf_op jit(solution)/shard_map/ppermute | solution.py:27
  61.8 5.0 %copy-start = (bf16[128,7680]{1,0:T(8,128)(2,1)S(1)}, bf16[128,7680]{1,0:T(8,128)(2,1)}, u32[]{:S(2)}) copy-start(bf16[128,7680]{1,0:T(8,128)(2,1)} %param.7) | copy-start | bytes 5898244
  66.7 1.5 copy-start.6
  93.5 10.9 %collective-permute-start.1 = (bf16[1,2,128,768]{3,2,1,0:T(8,128)(2,1)}, bf16[1,2,128,768]{3,2,1,0:T(8,128)(2,1)S(1)}, u32[]{:S(2)}, u32[]{:S(2)}) collective-permute-start(bf16[1,2,128,768]{3,2,1,0:T(8,128)(2,1)} %bitcast.95), channel_id=1, source_target_pairs={{0,1},{1,2},{2,3},{3,16},{16,17},{17,18},{18,19},{19,0},{4,5},{5,6... | collective-permute-start | bytes 1179656 | tf_op jit(solution)/shard_map/ppermute | solution.py:105
  104.4 0.7 copy-start.1
  105.2 12.4 %collective-permute-start.2 = (bf16[1,2,128,768]{3,2,1,0:T(8,128)(2,1)S(1)}, bf16[1,2,128,768]{3,2,1,0:T(8,128)(2,1)S(1)}, u32[]{:S(2)}, u32[]{:S(2)}) collective-permute-start(bf16[1,2,128,768]{3,2,1,0:T(8,128)(2,1)S(1)} %collective-permute-done.1), channel_id=1, source_target_pairs={{0,1},{1,2},{2,3},{3,16},{16,17},{17,18},{18,19},{19,0},{4,5},{5,6... | collective-permute-start | bytes 1179656 | tf_op jit(solution)/shard_map/ppermute | solution.py:105
  105.2 12.4 %collective-permute-start.5 = (bf16[1,2,128,768]{3,2,1,0:T(8,128)(2,1)}, bf16[1,2,128,768]{3,2,1,0:T(8,128)(2,1)S(1)}, u32[]{:S(2)}, u32[]{:S(2)}) collective-permute-start(bf16[1,2,128,768]{3,2,1,0:T(8,128)(2,1)} %bitcast.96), channel_id=1, source_target_pairs={{1,0},{2,1},{3,2},{16,3},{17,16},{18,17},{19,18},{0,19},{5,4},{6,5... | collective-permute-start | bytes 1179656 | tf_op jit(solution)/shard_map/ppermute | solution.py:107
  117.5 12.9 %copy-start.3 = (bf16[1,2,128,768]{3,2,1,0:T(8,128)(2,1)}, bf16[1,2,128,768]{3,2,1,0:T(8,128)(2,1)S(1)}, u32[]{:S(2)}) copy-start(bf16[1,2,128,768]{3,2,1,0:T(8,128)(2,1)S(1)} %collective-permute-done.2) | copy-start | bytes 1179652
  117.5 8.2 %collective-permute-start.3 = (bf16[1,2,128,768]{3,2,1,0:T(8,128)(2,1)S(1)}, bf16[1,2,128,768]{3,2,1,0:T(8,128)(2,1)S(1)}, u32[]{:S(2)}, u32[]{:S(2)}) collective-permute-start(bf16[1,2,128,768]{3,2,1,0:T(8,128)(2,1)S(1)} %collective-permute-done.2), channel_id=1, source_target_pairs={{0,1},{1,2},{2,3},{3,16},{16,17},{17,18},{18,19},{19,0},{4,5},{5,6... | collective-permute-start | bytes 1179656 | tf_op jit(solution)/shard_map/ppermute | solution.py:105
  117.6 12.9 %copy-start.2 = (bf16[1,2,128,768]{3,2,1,0:T(8,128)(2,1)}, bf16[1,2,128,768]{3,2,1,0:T(8,128)(2,1)S(1)}, u32[]{:S(2)}) copy-start(bf16[1,2,128,768]{3,2,1,0:T(8,128)(2,1)S(1)} %collective-permute-done.5) | copy-start | bytes 1179652
  117.6 10.2 %collective-permute-start.6 = (bf16[1,2,128,768]{3,2,1,0:T(8,128)(2,1)S(1)}, bf16[1,2,128,768]{3,2,1,0:T(8,128)(2,1)}, u32[]{:S(2)}, u32[]{:S(2)}) collective-permute-start(bf16[1,2,128,768]{3,2,1,0:T(8,128)(2,1)S(1)} %collective-permute-done.5), channel_id=1, source_target_pairs={{1,0},{2,1},{3,2},{16,3},{17,16},{18,17},{19,18},{0,19},{5,4},{6,5... | collective-permute-start | bytes 1179656 | tf_op jit(solution)/shard_map/ppermute | solution.py:107
  125.8 4.7 %copy-start.4 = (bf16[1,2,128,768]{3,2,1,0:T(8,128)(2,1)}, bf16[1,2,128,768]{3,2,1,0:T(8,128)(2,1)S(1)}, u32[]{:S(2)}) copy-start(bf16[1,2,128,768]{3,2,1,0:T(8,128)(2,1)S(1)} %collective-permute-done.3) | copy-start | bytes 1179652
  125.8 12.4 %collective-permute-start.4 = (bf16[1,2,128,768]{3,2,1,0:T(8,128)(2,1)S(1)}, bf16[1,2,128,768]{3,2,1,0:T(8,128)(2,1)}, u32[]{:S(2)}, u32[]{:S(2)}) collective-permute-start(bf16[1,2,128,768]{3,2,1,0:T(8,128)(2,1)S(1)} %collective-permute-done.3), channel_id=1, source_target_pairs={{0,1},{1,2},{2,3},{3,16},{16,17},{17,18},{18,19},{19,0},{4,5},{5,6... | collective-permute-start | bytes 1179656 | tf_op jit(solution)/shard_map/ppermute | solution.py:105
  127.8 17.6 %collective-permute-start.7 = (bf16[1,2,128,768]{3,2,1,0:T(8,128)(2,1)}, bf16[1,2,128,768]{3,2,1,0:T(8,128)(2,1)S(1)}, u32[]{:S(2)}, u32[]{:S(2)}) collective-permute-start(bf16[1,2,128,768]{3,2,1,0:T(8,128)(2,1)} %collective-permute-done.6), channel_id=1, source_target_pairs={{1,0},{2,1},{3,2},{16,3},{17,16},{18,17},{19,18},{0,19},{5,4},{6,5... | collective-permute-start | bytes 1179656 | tf_op jit(solution)/shard_map/ppermute | solution.py:107
  139.2 24.4 %copy-start.5 = (s32[1,1,4,2]{2,3,1,0:T(2,128)S(1)}, s32[1,1,4,2]{2,3,1,0:T(2,128)}, u32[]{:S(2)}) copy-start(s32[1,1,4,2]{2,3,1,0:T(2,128)} %param.9) | copy-start | bytes 100
Sparse Core Ops, SparseCore 0:
  93.7 69.8 all-gather.2
